TPU v7x, 512 devices: a whole 4x4x16 slice. The times are simulated.
512 devices in a mesh: dp: 64 (over y, z), tensor: 8 (over x, core).
Axes of the slice: x: 4, y: 4, z: 16, core: 2. Of those that a mesh axis runs over, the one named last changes fastest.
Arguments:
- tokens: bfloat16 [65536, 1408], P(('dp', 'tensor')), may hold values from -6 to 6
- ln1_gain: float32 [1408], replicated, may hold values from 0.1 to 1.9
- ln1_shift: float32 [1408], replicated, may hold values from -3 to 3
- w_qkv: bfloat16 [1408, 16, 264], P(None, 'tensor')
- w_out: bfloat16 [16, 88, 1408], P('tensor'), may hold values from -0.625 to 0.625
- ln2_gain: float32 [1408], replicated, may hold values from 0.1 to 1.9
- ln2_shift: float32 [1408], replicated, may hold values from -3 to 3
- w_proj: bfloat16 [5632, 3584], P('dp', 'tensor'), may hold values from -0.078125 to 0.078125
- proj_bias: float32 [3584], P('tensor'), may hold values from -3 to 3
- segments: int32 [64, 256], P('dp'), may hold values from 0 to 7, never falling along the last dimension, each value on 1 to 128 neighbouring positions
- owners: int32 [16384, 1], P('dp'), may hold values from 0 to 63; in each aligned block of 256 rows (0 to 255, 256 to 511, ...) at most 8 rows name the same one
Outputs:
- delivered: bfloat16 [32768, 3584], P('dp', 'tensor')
Inputs may be any that keep to these rules, and one draw needn't show every extreme that they name: `segments`: within a pack numbers never fall, every image has 1 to 128 groups and one has exactly that many. `owners`: among the 256 merged tokens of one pack no owner gets more than 8; in some pack an owner gets exactly 8.
All inputs are finite; a program needn't handle non-finite values.
Results may differ from a plain program's by a relative error of at most 0.015.
Values may be sent and summed in bfloat16 or wider, within the bound.
No kernel may reach another device: no remote copies, remote signals or barrier semaphores. Data moves between devices by JAX's collectives and lax.ppermute only.
A program may use at most 64 MiB of HBM per device.

v0:
```python
import jax
import jax.numpy as jnp
from jax import lax
from jax.sharding import PartitionSpec as P


def layer_norm(values, gain, shift):
    wide = values.astype(jnp.float32)
    average = jnp.mean(wide, axis=-1, keepdims=True)
    centred = wide - average
    variance = jnp.mean(centred * centred, axis=-1, keepdims=True)
    return centred * lax.rsqrt(variance + 1e-06) * gain + shift


def attend(heads_qkv, token_segs):
    row_count = heads_qkv.shape[0]
    width = heads_qkv.shape[2] // 3
    queries = heads_qkv[:, :, :width]
    keys_all = heads_qkv[:, :, width : 2 * width]
    values_all = heads_qkv[:, :, 2 * width :]
    score_scale = 1.0 / jnp.sqrt(jnp.float32(width))
    block_rows = min(512, row_count)
    outputs = []
    for block_index in range(row_count // block_rows):
        lower = block_index * block_rows
        scores = (
            jnp.einsum(
                "qhd,khd->hqk",
                queries[lower : lower + block_rows],
                keys_all,
                preferred_element_type=jnp.float32,
            )
            * score_scale
        )
        same = token_segs[lower : lower + block_rows][:, None] == token_segs[None, :]
        scores = jnp.where(same[None], scores, -jnp.inf)
        row_max = jnp.max(scores, axis=-1, keepdims=True)
        exponent = jnp.exp(scores - row_max)
        probs = (exponent / jnp.sum(exponent, axis=-1, keepdims=True)).astype(jnp.bfloat16)
        context = jnp.einsum("hqk,khd->qhd", probs, values_all, preferred_element_type=jnp.float32)
        outputs.append(context.astype(jnp.bfloat16))
    return jnp.concatenate(outputs, axis=0)


def shards(
    tokens,
    ln1_gain,
    ln1_shift,
    w_qkv,
    w_out,
    ln2_gain,
    ln2_shift,
    w_proj,
    proj_bias,
    segments,
    owners,
):
    dp_count = lax.axis_size("dp")
    tp_count = lax.axis_size("tensor")
    w_proj_all = lax.all_gather(w_proj, "dp", axis=0, tiled=True)
    w_out_all = lax.all_gather(w_out, "tensor", axis=0, tiled=True)
    gathered = lax.all_gather(tokens, "tensor", axis=0, tiled=True)
    row_count = gathered.shape[0]
    local_rows = tokens.shape[0]
    normed = layer_norm(gathered, ln1_gain, ln1_shift).astype(jnp.bfloat16)
    heads_here = w_qkv.shape[1]
    heads_qkv = jnp.dot(
        normed, w_qkv.reshape(w_qkv.shape[0], -1), preferred_element_type=jnp.float32
    )
    heads_qkv = heads_qkv.astype(jnp.bfloat16).reshape(row_count, heads_here, -1)
    token_segs = jnp.repeat(segments[0], 4)
    context = attend(heads_qkv, token_segs).reshape(tp_count, local_rows, -1)
    context_mine = lax.all_to_all(context, "tensor", split_axis=0, concat_axis=0, tiled=True)
    out_heads = w_out_all.reshape(tp_count, -1, w_out_all.shape[2])
    attn = jnp.einsum("sqd,sdo->qo", context_mine, out_heads, preferred_element_type=jnp.float32)
    hidden = (tokens.astype(jnp.float32) + attn).astype(jnp.bfloat16)
    normed_two = layer_norm(hidden, ln2_gain, ln2_shift).astype(jnp.bfloat16)
    merged_mine = normed_two.reshape(local_rows // 4, -1)
    merged = lax.all_gather(merged_mine, "tensor", axis=0, tiled=True)
    groups = merged.shape[0]
    summed = jnp.dot(merged, w_proj_all, preferred_element_type=jnp.float32)
    projected = (summed + proj_bias).astype(jnp.bfloat16)
    dests = owners[:, 0]
    onehot = (dests[:, None] == jnp.arange(dp_count, dtype=jnp.int32)[None, :]).astype(jnp.int32)
    earlier = jnp.cumsum(onehot, axis=0) - onehot
    position = jnp.sum(earlier * onehot, axis=1)
    capacity = 2 * groups // dp_count
    slot_index = dests * capacity + position
    scatter_table = (
        slot_index[None, :] == jnp.arange(dp_count * capacity, dtype=jnp.int32)[:, None]
    ).astype(jnp.bfloat16)
    outgoing = jnp.dot(scatter_table, projected, preferred_element_type=jnp.float32).astype(
        jnp.bfloat16
    )
    outgoing = outgoing.reshape(dp_count, capacity, -1)
    arrived = lax.all_to_all(outgoing, "dp", split_axis=0, concat_axis=0, tiled=True)
    return arrived.reshape(dp_count * capacity, -1)


def solution(mesh):
    return jax.shard_map(
        shards,
        mesh=mesh,
        in_specs=(
            P(("dp", "tensor"), None),
            P(),
            P(),
            P(None, "tensor", None),
            P("tensor", None, None),
            P(),
            P(),
            P("dp", "tensor"),
            P("tensor"),
            P("dp", None),
            P("dp", None),
        ),
        out_specs=P("dp", "tensor"),
        check_vma=False,
    )
```

profile of v0, /device:TPU:8, one launch (start us, length us, event | category | flops | bytes accessed | tf_op | source)
XLA Modules:
  0.0 339.7 jit_solution(10978495204272725188)
XLA Ops:
  6.5 0.7 all-gather.5.cloned.1.call-update
  7.3 0.7 all-gather.7.cloned.1.call-update
  8.1 0.7 all-gather.11.cloned.1.call-update
  8.8 0.7 slice_bitcast_fusion.1
  9.7 0.1 eq.89
  9.9 0.8 broadcast_in_dim.25
  10.6 0.1 eq.86
  10.8 0.7 broadcast_compare_fusion.1
  11.4 36.8 %all-gather.5.cloned.1.call-done = bf16[1024,1408]{1,0:T(8,128)(2,1)} async-done(((bf16[128,1408]{1,0:T(8,128)(2,1)}), bf16[1024,1408]{1,0:T(8,128)(2,1)}) %all-gather.5.cloned.1.call-update) | async-done | bytes 2883600 | tf_op jit(solution)/shard_map/all_gather | solution.py:62
  48.2 2.4 convert_reduce_fusion
  50.6 0.3 copy-done.1
  50.9 0.9 fusion.4
  51.8 3.1 fusion.27
  55.0 4.8 %fusion.82 = (f32[2,512]{1,0:T(2,128)S(1)}, f32[2,512,1024]{2,1,0:T(8,128)}) fusion(pred[512,1024]{1,0:T(8,128)(4,1)S(1)} %get-tuple-element.5, bf16[1024,2,264]{0,2,1:T(8,128)(2,1)} %bitcast.63), kind=kOutput, calls=%fused_computation.86 | convolution fusion | flops 188744704 | bytes 5263360 | tf_op jit(solution)/shard_map/sub | solution.py:38
  59.8 4.8 %fusion.73 = (f32[2,512]{1,0:T(2,128)S(1)}, f32[2,512,1024]{2,1,0:T(8,128)}) fusion(pred[512,1024]{1,0:T(8,128)(4,1)S(1)} %get-tuple-element.6, bf16[1024,2,264]{0,2,1:T(8,128)(2,1)} %bitcast.64), kind=kOutput, calls=%fused_computation.85 | convolution fusion | flops 188744704 | bytes 5263360 | tf_op jit(solution)/shard_map/sub | solution.py:38
  64.6 3.2 fusion.33
  67.8 0.4 copy-done.10
  68.2 0.9 fusion.34
  69.3 16.0 %all_to_all.10 = bf16[8,128,176]{1,2,0:T(8,128)(2,1)S(1)} all-to-all(bf16[8,128,176]{1,2,0:T(8,128)(2,1)S(1)} %copy.18), channel_id=1, replica_groups=mesh['dp'=64,'tensor'=8] {'tensor'}, dimensions={0} | all-to-all | bytes 720896 | tf_op jit(solution)/shard_map/all_to_all | solution.py:73
  85.2 8.4 %all-gather.7.cloned.1.call-done = bf16[16,88,1408]{2,1,0:T(8,128)(2,1)} async-done(((bf16[2,88,1408]{2,1,0:T(8,128)(2,1)}), bf16[16,88,1408]{2,1,0:T(8,128)(2,1)}) %all-gather.7.cloned.1.call-update) | async-done | bytes 3964944 | tf_op jit(solution)/shard_map/all_gather | solution.py:61
  93.7 3.0 fusion.91
  96.7 0.2 multiply_reduce_fusion
  96.9 0.2 add_convert_fusion
  97.1 1.0 reshape.155
  98.2 0.6 reduce-window.6
  98.8 0.2 slice_reduce_fusion
  99.1 146.7 %all-gather.11.cloned.1.call-done = bf16[5632,448]{1,0:T(8,128)(2,1)} async-done(((bf16[88,448]{1,0:T(8,128)(2,1)}), bf16[5632,448]{1,0:T(8,128)(2,1)}) %all-gather.11.cloned.1.call-update) | async-done | bytes 5046288 | tf_op jit(solution)/shard_map/all_gather | solution.py:60
  245.8 32.5 %all-gather.9.cloned.1.call-done = bf16[256,5632]{1,0:T(8,128)(2,1)} async-done(((bf16[32,5632]{1,0:T(8,128)(2,1)}), bf16[256,5632]{1,0:T(8,128)(2,1)}) %all-gather.9.cloned.1.call-update) | async-done | bytes 2883600 | tf_op jit(solution)/shard_map/all_gather | solution.py:79
  278.3 6.0 %convolution_convert_fusion = bf16[512,448]{0,1:T(8,128)(2,1)S(1)} fusion(bf16[256,5632]{1,0:T(8,128)(2,1)} %all-gather.9.cloned.1.call-done, bf16[5632,448]{1,0:T(8,128)(2,1)} %all-gather.11.cloned.1.call-done, s32[256]{0:T(256)S(1)} %multiply_add_fusion, f32[448]{0:T(512)S(1)} %copy-done.8), kind=kOutput, calls=%fused_computation.36 | convolution fusion | flops 1409875968 | bytes 8391424 | tf_op jit(solution)/shard_map/dot_general | solution.py:92
  284.3 0.2 copy.19
  284.5 47.7 %all_to_all.11 = bf16[64,8,448]{2,1,0:T(8,128)(2,1)S(1)} all-to-all(bf16[64,8,448]{2,1,0:T(8,128)(2,1)S(1)} %bitcast.55), channel_id=1, replica_groups=mesh['dp'=64,'tensor'=8] {'dp'}, dimensions={0} | all-to-all | bytes 917504 | tf_op jit(solution)/shard_map/all_to_all | solution.py:96
  332.2 1.0 copy.20
  (40 shorter events, 0.8 us)
Async XLA Ops:
  6.5 45.3 %copy-start = (bf16[1408,2,264]{0,2,1:T(8,128)(2,1)S(1)}, bf16[1408,2,264]{0,2,1:T(8,128)(2,1)}, u32[]{:S(2)}) copy-start(bf16[1408,2,264]{0,2,1:T(8,128)(2,1)} %param.14) | copy-start | bytes 4460548
  6.5 45.3 %copy-start.7 = (f32[1408]{0:T(1024)S(1)}, f32[1408]{0:T(1024)}, u32[]{:S(2)}) copy-start(f32[1408]{0:T(1024)} %param.12) | copy-start | bytes 16900
  6.5 45.3 %copy-start.6 = (f32[1408]{0:T(1024)S(1)}, f32[1408]{0:T(1024)}, u32[]{:S(2)}) copy-start(f32[1408]{0:T(1024)} %param.13) | copy-start | bytes 16900
  6.5 41.7 %all-gather.5.cloned.1.call-start = ((), (), s32[]{:S(2)}) async-start(), calls=%async_computation.2 | async-start | bytes 3244032 | tf_op jit(solution)/shard_map/all_gather | solution.py:62
  7.3 86.4 %all-gather.7.cloned.1.call-start = ((), (), s32[]{:S(2)}) async-start(), calls=%async_computation.3 | async-start | bytes 4460544 | tf_op jit(solution)/shard_map/all_gather | solution.py:61
  8.0 237.8 %all-gather.11.cloned.1.call-start = ((), (), s32[]{:S(2)}) async-start(), calls=%async_computation.5 | async-start | bytes 5857280 | tf_op jit(solution)/shard_map/all_gather | solution.py:60
  8.7 269.5 %all-gather.9.cloned.1.call-start = ((), (), s32[]{:S(2)}) async-start(), calls=%async_computation.4 | async-start | bytes 3244032 | tf_op jit(solution)/shard_map/all_gather | solution.py:79
  48.2 2.7 copy-start.1
  59.8 4.8 %copy-start.9 = (bf16[1024,528]{0,1:T(8,128)(2,1)S(1)}, bf16[1024,528]{0,1:T(8,128)(2,1)}, u32[]{:S(2)}) copy-start(bf16[1024,528]{0,1:T(8,128)(2,1)} %fusion.27) | copy-start | bytes 3244036
  64.6 3.6 %copy-start.10 = (f32[2,512,1024]{2,1,0:T(8,128)S(1)}, f32[2,512,1024]{2,1,0:T(8,128)}, u32[]{:S(2)}) copy-start(f32[2,512,1024]{2,1,0:T(8,128)} %get-tuple-element.10) | copy-start | bytes 12582916
  68.2 25.5 %copy-start.2 = (bf16[128,1408]{1,0:T(8,128)(2,1)S(1)}, bf16[128,1408]{1,0:T(8,128)(2,1)}, u32[]{:S(2)}) copy-start(bf16[128,1408]{1,0:T(8,128)(2,1)} %param.11) | copy-start | bytes 1081348
  69.1 27.8 %copy-start.4 = (f32[1408]{0:T(1024)S(1)}, f32[1408]{0:T(1024)}, u32[]{:S(2)}) copy-start(f32[1408]{0:T(1024)} %param.17) | copy-start | bytes 16900
  69.1 27.8 %copy-start.5 = (f32[1408]{0:T(1024)S(1)}, f32[1408]{0:T(1024)}, u32[]{:S(2)}) copy-start(f32[1408]{0:T(1024)} %param.16) | copy-start | bytes 16900
  85.2 12.9 %copy-start.3 = (s32[256,1]{0,1:T(1,128)S(1)}, s32[256,1]{0,1:T(1,128)}, u32[]{:S(2)}) copy-start(s32[256,1]{0,1:T(1,128)} %param.21) | copy-start | bytes 3076
  93.7 184.6 %copy-start.8 = (f32[448]{0:T(512)S(1)}, f32[448]{0:T(512)}, u32[]{:S(2)}) copy-start(f32[448]{0:T(512)} %param.19) | copy-start | bytes 5380
Sparse Core Ops, SparseCore 0:
  9.5 38.6 all-gather.4
  50.3 43.2 all-gather.6
  96.6 149.1 all-gather.10
  247.8 30.4 all-gather.8
where the time goes:
time: 340 us
  waiting for transfers between devices  226 us (66%)
  blocking collectives  63.7 us (19%)
  matrix products  25.8 us (8%)
  between operations  13.3 us (4%)
  other arithmetic  5.21 us (2%)
  local copies, waits for them, and re-layouts  5.09 us (1%)
    all_gather x1, waiting for transfers between devices, shards(): w_proj_all = lax.all_gather(w_proj, 'dp', axis=0, tiled=True)  147 us
    all_to_all x1, blocking collectives, shards(): lax.all_to_all(outgoing, 'dp', split_axis=0, concat_axis=0, tiled=True)  47.7 us
    all_gather x1, waiting for transfers between devices, shards(): gathered = lax.all_gather(tokens, 'tensor', axis=0, tiled=True)  36.8 us
    all_gather x1, waiting for transfers between devices, shards(): merged = lax.all_gather(merged_mine, 'tensor', axis=0, tiled=True)  32.5 us
    all_to_all x1, blocking collectives, shards(): lax.all_to_all(context, 'tensor', split_axis=0, concat_axis=0, tiled=True)  16 us
    sub x2, matrix products, attend(): exponent = jnp.exp(scores - row_max)  9.62 us
    all_gather x1, waiting for transfers between devices, shards(): w_out_all = lax.all_gather(w_out, 'tensor', axis=0, tiled=True)  8.44 us
  transfers between devices with their start and end apart: 4, of which 4 were waited for; matrix products, arithmetic and copies ran while one was open for 8% of the time, Pallas kernels for 0%

commit v1 on v0

--- a/solution.py
+++ b/solution.py
@@ -59,7 +59,8 @@
     tp_count = lax.axis_size("tensor")
     w_proj_all = lax.all_gather(w_proj, "dp", axis=0, tiled=True)
     w_out_all = lax.all_gather(w_out, "tensor", axis=0, tiled=True)
-    gathered = lax.all_gather(tokens, "tensor", axis=0, tiled=True)
+    outgoing_2 = jnp.stack([tokens] * lax.axis_size("tensor"))
+    gathered = jnp.concatenate(lax.all_to_all(outgoing_2, "tensor", 0, 0), axis=0)
     row_count = gathered.shape[0]
     local_rows = tokens.shape[0]
     normed = layer_norm(gathered, ln1_gain, ln1_shift).astype(jnp.bfloat16)

time: 340 us -> 315 us (0.926)
  waiting for transfers between devices: 226 us -> 197 us
  blocking collectives: 63.7 us -> 58.7 us
  other arithmetic: 5.21 us -> 9.83 us
  starting transfers between devices: 0.12 us -> 4.5 us
    all_to_all x0 -> x1, waiting for transfers between devices: none -> 50 us  [shards(): lax.all_to_all(outgoing_2, 'tensor', 0, 0)]
    all_gather x1 -> x0, waiting for transfers between devices: 36.8 us -> none  [shards(): gathered = lax.all_gather(tokens, 'tensor', axis=0, tiled=True)]
    all_gather x1, waiting for transfers between devices: 147 us -> 113 us  [shards(): w_proj_all = lax.all_gather(w_proj, 'dp', axis=0, tiled=True)]
    all_gather x1, waiting for transfers between devices: 8.44 us -> 0.01 us  [shards(): w_out_all = lax.all_gather(w_out, 'tensor', axis=0, tiled=True)]
    all_to_all x1, blocking collectives: 16 us -> 11 us  [shards(): lax.all_to_all(context, 'tensor', split_axis=0, concat_axis=0, tiled=True)]
    all_to_all x0 -> x1, starting transfers between devices: none -> 4.42 us  [shards(): lax.all_to_all(outgoing_2, 'tensor', 0, 0)]
  transfers between devices with their start and end apart: 4 -> 4, of which waited for: 4 -> 3; matrix products, arithmetic and copies ran while one was open for 8% -> 11% of each run, Pallas kernels for 0% -> 0%
where the time goes in v1:
time: 315 us
  waiting for transfers between devices  197 us (63%)
  blocking collectives  58.7 us (19%)
  matrix products  25.6 us (8%)
  between operations  13.3 us (4%)
  other arithmetic  9.83 us (3%)
  local copies, waits for them, and re-layouts  6.21 us (2%)
  starting transfers between devices  4.5 us (1%)
    all_gather x1, waiting for transfers between devices, shards(): w_proj_all = lax.all_gather(w_proj, 'dp', axis=0, tiled=True)  113 us
    all_to_all x1, waiting for transfers between devices, shards(): lax.all_to_all(outgoing_2, 'tensor', 0, 0)  50 us
    all_to_all x1, blocking collectives, shards(): lax.all_to_all(outgoing, 'dp', split_axis=0, concat_axis=0, tiled=True)  47.7 us
    all_gather x1, waiting for transfers between devices, shards(): merged = lax.all_gather(merged_mine, 'tensor', axis=0, tiled=True)  32.6 us
    all_to_all x1, blocking collectives, shards(): lax.all_to_all(context, 'tensor', split_axis=0, concat_axis=0, tiled=True)  11 us
    sub x2, matrix products, attend(): exponent = jnp.exp(scores - row_max)  9.62 us
  transfers between devices with their start and end apart: 4, of which 3 were waited for; matrix products, arithmetic and copies ran while one was open for 11% of the time, Pallas kernels for 0%

profile of v1, /device:TPU:8, one launch (start us, length us, event | category | flops | bytes accessed | tf_op | source)
XLA Modules:
  0.0 314.8 jit_solution(6597091328763344059)
XLA Ops:
  6.5 0.7 all-gather.4.cloned.1.call-update
  7.3 0.7 all-gather.8.cloned.1.call-update
  8.0 2.9 stack.2
  10.9 4.4 %all-to-all-start = ((bf16[8,128,1408]{2,1,0:T(8,128)(2,1)}), bf16[8,128,1408]{2,1,0:T(8,128)(2,1)}, u32[]{:S(2)}, u32[]{:S(2)}) async-start(bf16[8,128,1408]{2,1,0:T(8,128)(2,1)} %stack.2), calls=%async_computation | async-start | bytes 5767168 | tf_op jit(solution)/shard_map/all_to_all | solution.py:63
  15.5 0.1 eq.84
  15.7 0.1 eq.89
  15.9 0.1 eq.86
  16.0 0.7 broadcast_compare_fusion.1
  16.7 50.0 %all-to-all-done = bf16[8,128,1408]{2,1,0:T(8,128)(2,1)} async-done(((bf16[8,128,1408]{2,1,0:T(8,128)(2,1)}), bf16[8,128,1408]{2,1,0:T(8,128)(2,1)}, u32[]{:S(2)}, u32[]{:S(2)}) %all-to-all-start) | async-done | bytes 2883616 | tf_op jit(solution)/shard_map/all_to_all | solution.py:63
  66.7 2.3 convert_reduce_fusion
  69.0 2.7 fusion.4
  71.8 2.9 fusion.7
  74.7 2.9 convolution_convert_fusion
  77.6 4.8 %fusion.73 = (f32[2,512]{1,0:T(2,128)S(1)}, f32[2,512,1024]{2,1,0:T(8,128)}) fusion(pred[512,1024]{1,0:T(8,128)(4,1)S(1)} %get-tuple-element.5, bf16[1024,2,264]{0,2,1:T(8,128)(2,1)} %bitcast.66), kind=kOutput, calls=%fused_computation.81 | convolution fusion | flops 188744704 | bytes 5263360 | tf_op jit(solution)/shard_map/sub | solution.py:38
  82.4 4.8 %fusion.64 = (f32[2,512]{1,0:T(2,128)S(1)}, f32[2,512,1024]{2,1,0:T(8,128)}) fusion(pred[512,1024]{1,0:T(8,128)(4,1)S(1)} %get-tuple-element.6, bf16[1024,2,264]{0,2,1:T(8,128)(2,1)} %bitcast.67), kind=kOutput, calls=%fused_computation.80 | convolution fusion | flops 188744704 | bytes 5263360 | tf_op jit(solution)/shard_map/sub | solution.py:38
  87.2 3.2 %fusion.24 = bf16[512,2,88]{0,2,1:T(8,128)(2,1)S(1)} fusion(f32[2,512,1024]{2,1,0:T(8,128)} %get-tuple-element.12, f32[2,512]{1,0:T(2,128)S(1)} %get-tuple-element.11, bf16[1024,2,264]{0,2,1:T(8,128)(2,1)S(1)} %bitcast.68), kind=kOutput, calls=%fused_computation.36 | convolution fusion | flops 186736640 | bytes 4739072 | tf_op jit(solution)/shard_map/hqk,khd->qhd/dot_general | solution.py:40
  90.5 0.2 copy-done.10
  90.7 0.9 fusion.25
  91.8 11.0 %all_to_all.15 = bf16[8,128,176]{1,2,0:T(8,128)(2,1)S(1)} all-to-all(bf16[8,128,176]{1,2,0:T(8,128)(2,1)S(1)} %copy.22), channel_id=1, replica_groups=mesh['dp'=64,'tensor'=8] {'tensor'}, dimensions={0} | all-to-all | bytes 720896 | tf_op jit(solution)/shard_map/all_to_all | solution.py:74
  102.8 3.0 fusion.82
  105.8 0.2 multiply_reduce_fusion
  106.1 0.2 add_convert_fusion
  106.3 1.0 reshape.190
  107.3 0.6 reduce-window.6
  107.9 0.2 slice_reduce_fusion
  108.1 0.1 fusion.58
  108.2 112.5 %all-gather.8.cloned.1.call-done = bf16[5632,448]{1,0:T(8,128)(2,1)} async-done(((bf16[88,448]{1,0:T(8,128)(2,1)}), bf16[5632,448]{1,0:T(8,128)(2,1)}) %all-gather.8.cloned.1.call-update) | async-done | bytes 5046288 | tf_op jit(solution)/shard_map/all_gather | solution.py:60
  220.8 32.6 %all-gather.6.cloned.1.call-done = bf16[256,5632]{1,0:T(8,128)(2,1)} async-done(((bf16[32,5632]{1,0:T(8,128)(2,1)}), bf16[256,5632]{1,0:T(8,128)(2,1)}) %all-gather.6.cloned.1.call-update) | async-done | bytes 2883600 | tf_op jit(solution)/shard_map/all_gather | solution.py:80
  253.4 6.0 %convolution_convert_fusion.1 = bf16[512,448]{0,1:T(8,128)(2,1)S(1)} fusion(bf16[256,5632]{1,0:T(8,128)(2,1)} %all-gather.6.cloned.1.call-done, bf16[5632,448]{1,0:T(8,128)(2,1)} %all-gather.8.cloned.1.call-done, s32[256]{0:T(256)S(1)} %multiply_add_fusion, f32[448]{0:T(512)S(1)} %copy-done.8), kind=kOutput, calls=%fused_computation.31 | convolution fusion | flops 1409875968 | bytes 8391424 | tf_op jit(solution)/shard_map/dot_general | solution.py:93
  259.4 0.2 copy.23
  259.6 47.7 %all_to_all.16 = bf16[64,8,448]{2,1,0:T(8,128)(2,1)S(1)} all-to-all(bf16[64,8,448]{2,1,0:T(8,128)(2,1)S(1)} %bitcast.58), channel_id=1, replica_groups=mesh['dp'=64,'tensor'=8] {'dp'}, dimensions={0} | all-to-all | bytes 917504 | tf_op jit(solution)/shard_map/all_to_all | solution.py:97
  307.3 1.0 copy.24
  (41 shorter events, 0.6 us)
Async XLA Ops:
  6.5 68.2 %copy-start = (bf16[1408,2,264]{0,2,1:T(8,128)(2,1)S(1)}, bf16[1408,2,264]{0,2,1:T(8,128)(2,1)}, u32[]{:S(2)}) copy-start(bf16[1408,2,264]{0,2,1:T(8,128)(2,1)} %param.14) | copy-start | bytes 4460548
  6.5 96.2 %all-gather.4.cloned.1.call-start = ((), (), s32[]{:S(2)}) async-start(), calls=%async_computation.3 | async-start | bytes 4460544 | tf_op jit(solution)/shard_map/all_gather | solution.py:61
  7.3 213.5 %all-gather.8.cloned.1.call-start = ((), (), s32[]{:S(2)}) async-start(), calls=%async_computation.5 | async-start | bytes 5857280 | tf_op jit(solution)/shard_map/all_gather | solution.py:60
  8.0 7.4 %copy-start.7 = (s32[1,256]{1,0:T(1,128)S(1)}, s32[1,256]{1,0:T(1,128)}, u32[]{:S(2)}) copy-start(s32[1,256]{1,0:T(1,128)} %param.20) | copy-start | bytes 3076
  10.9 55.8 %all-to-all-start = ((bf16[8,128,1408]{2,1,0:T(8,128)(2,1)}), bf16[8,128,1408]{2,1,0:T(8,128)(2,1)}, u32[]{:S(2)}, u32[]{:S(2)}) async-start(bf16[8,128,1408]{2,1,0:T(8,128)(2,1)} %stack.2), calls=%async_computation | async-start | bytes 5767168 | tf_op jit(solution)/shard_map/all_to_all | solution.py:63
  15.3 56.4 %copy-start.3 = (f32[1408]{0:T(1024)S(1)}, f32[1408]{0:T(1024)}, u32[]{:S(2)}) copy-start(f32[1408]{0:T(1024)} %param.13) | copy-start | bytes 16900
  15.3 56.4 %copy-start.4 = (f32[1408]{0:T(1024)S(1)}, f32[1408]{0:T(1024)}, u32[]{:S(2)}) copy-start(f32[1408]{0:T(1024)} %param.12) | copy-start | bytes 16900
  15.3 238.1 %all-gather.6.cloned.1.call-start = ((), (), s32[]{:S(2)}) async-start(), calls=%async_computation.4 | async-start | bytes 3244032 | tf_op jit(solution)/shard_map/all_gather | solution.py:80
  82.4 4.8 %copy-start.9 = (bf16[1024,528]{0,1:T(8,128)(2,1)S(1)}, bf16[1024,528]{0,1:T(8,128)(2,1)}, u32[]{:S(2)}) copy-start(bf16[1024,528]{0,1:T(8,128)(2,1)} %convolution_convert_fusion) | copy-start | bytes 3244036
  87.2 3.5 %copy-start.10 = (f32[2,512,1024]{2,1,0:T(8,128)S(1)}, f32[2,512,1024]{2,1,0:T(8,128)}, u32[]{:S(2)}) copy-start(f32[2,512,1024]{2,1,0:T(8,128)} %get-tuple-element.10) | copy-start | bytes 12582916
  90.7 12.0 %copy-start.1 = (bf16[128,1408]{1,0:T(8,128)(2,1)S(1)}, bf16[128,1408]{1,0:T(8,128)(2,1)}, u32[]{:S(2)}) copy-start(bf16[128,1408]{1,0:T(8,128)(2,1)} %param.11) | copy-start | bytes 1081348
  91.6 14.4 %copy-start.5 = (f32[1408]{0:T(1024)S(1)}, f32[1408]{0:T(1024)}, u32[]{:S(2)}) copy-start(f32[1408]{0:T(1024)} %param.17) | copy-start | bytes 16900
  91.6 14.4 %copy-start.6 = (f32[1408]{0:T(1024)S(1)}, f32[1408]{0:T(1024)}, u32[]{:S(2)}) copy-start(f32[1408]{0:T(1024)} %param.16) | copy-start | bytes 16900
  102.8 4.5 %copy-start.2 = (s32[256,1]{0,1:T(1,128)S(1)}, s32[256,1]{0,1:T(1,128)}, u32[]{:S(2)}) copy-start(s32[256,1]{0,1:T(1,128)} %param.21) | copy-start | bytes 3076
  102.8 150.6 %copy-start.8 = (f32[448]{0:T(512)S(1)}, f32[448]{0:T(512)}, u32[]{:S(2)}) copy-start(f32[448]{0:T(512)} %param.19) | copy-start | bytes 5380
Sparse Core Ops, SparseCore 0:
  9.5 58.5 all-gather.3
  71.0 149.6 all-gather.7
  222.9 30.4 all-gather.5
